TPU v7x, 128 devices: a whole 4x4x4 slice. The times are simulated.
128 devices in a mesh: grp: 8 (over z, core), dev: 16 (over y, x).
Axes of the slice: x: 4, y: 4, z: 4, core: 2. Of those that a mesh axis runs over, the one named last changes fastest.
Arguments:
- positions: float32 [3, 131072], P(None, ('grp', 'dev')), may hold values from -3 to 3
- velocities: float32 [3, 131072], P(None, ('grp', 'dev')), may hold values from -5 to 5
- accelerations: float32 [3, 131072], P(None, ('grp', 'dev')), may hold values from -3 to 3
- jerks: float32 [3, 131072], P(None, ('grp', 'dev')), may hold values from -3 to 3
- levels: int32 [131072], P(('grp', 'dev')), may hold values from 0 to 5
- counts: int32 [2, 128], replicated, may hold values from 1 to 256, 16384 in all within a row
- active_rows: int32 [2, 32768], P(None, ('grp', 'dev')), may hold values from 0 to 1023, as said below
Outputs:
- new_positions: float32 [3, 131072], P(None, ('grp', 'dev'))
- new_velocities: float32 [3, 131072], P(None, ('grp', 'dev'))
- new_accelerations: float32 [3, 131072], P(None, ('grp', 'dev'))
- new_jerks: float32 [3, 131072], P(None, ('grp', 'dev'))
Inputs may be any that keep to these rules, and one draw needn't show every extreme that they name: In each step the 128 counts sum to exactly 16384 and the largest of them is exactly 256. `active_rows`: for each step and device, the 256 entries of the device's slots are distinct indices of that device's own stars; only the first counts of them are live.
All inputs are finite; a program needn't handle non-finite values.
Results may differ from a plain program's by a relative error of at most 0.00022.
Values sent between devices are 32-bit elements; how exact they have to be, the bound alone decides.
No kernel may reach another device: no remote copies, remote signals or barrier semaphores. Data moves between devices by JAX's collectives and lax.ppermute only.
A program may use at most 128 MiB of HBM per device.

v0:
```python
import math
import jax
import jax.numpy as jnp
from jax import lax
from jax.sharding import PartitionSpec as P

tick_length = 1.0 / 128.0


def pair_block(targets, src_pos, src_vel, mass, soft_sq):
    gap_x = src_pos[0][None, :] - targets[0][:, None]
    gap_y = src_pos[1][None, :] - targets[1][:, None]
    gap_z = src_pos[2][None, :] - targets[2][:, None]
    drift_x = src_vel[0][None, :] - targets[3][:, None]
    drift_y = src_vel[1][None, :] - targets[4][:, None]
    drift_z = src_vel[2][None, :] - targets[5][:, None]
    squared = gap_x * gap_x + gap_y * gap_y + gap_z * gap_z + soft_sq
    inverse = lax.rsqrt(squared)
    weight = mass * inverse * inverse * inverse
    along = 3.0 * (gap_x * drift_x + gap_y * drift_y + gap_z * drift_z) * inverse * inverse
    return jnp.stack(
        [
            jnp.sum(weight * gap_x, axis=1),
            jnp.sum(weight * gap_y, axis=1),
            jnp.sum(weight * gap_z, axis=1),
            jnp.sum(weight * (drift_x - along * gap_x), axis=1),
            jnp.sum(weight * (drift_y - along * gap_y), axis=1),
            jnp.sum(weight * (drift_z - along * gap_z), axis=1),
        ]
    )


def block_terms(packed, src_pos, src_vel, mass, soft_sq):
    width, total = packed.shape
    block = math.gcd(total, 2048)
    grouped = packed.reshape(width, total // block, block).transpose(1, 0, 2)
    result = lax.map(lambda targets: pair_block(targets, src_pos, src_vel, mass, soft_sq), grouped)
    return result.transpose(1, 0, 2).reshape(width, total)


def predict(positions, velocities, accelerations, jerks, elapsed):
    span = elapsed[None, :]
    pred_pos = (
        positions
        + span * velocities
        + 0.5 * span * span * accelerations
        + span * span * span / 6.0 * jerks
    )
    pred_vel = velocities + span * accelerations + 0.5 * span * span * jerks
    return (pred_pos, pred_vel)


def correct(old_pos, old_vel, old_acc, old_jerk, force, jerk_new, span):
    span = span[None, :]
    new_vel = old_vel + 0.5 * span * (old_acc + force) + span * span / 12.0 * (old_jerk - jerk_new)
    new_pos = old_pos + 0.5 * span * (old_vel + new_vel) + span * span / 12.0 * (old_acc - force)
    return (new_pos, new_vel)


def shards(positions, velocities, accelerations, jerks, levels, counts, active_rows):
    devices_all = lax.axis_size("grp") * lax.axis_size("dev")
    my_rank = lax.axis_index("grp") * lax.axis_size("dev") + lax.axis_index("dev")
    star_dev = positions.shape[1]
    slot_cap = active_rows.shape[1]
    stars_all = star_dev * devices_all
    live_all = stars_all // 8
    mass = 1.0 / stars_all
    soft_sq = 0.0004 * (131072.0 / stars_all) ** (2.0 / 3.0)
    chunks = 4
    chunk = live_all // chunks
    last_time = -(jnp.left_shift(jnp.int32(1), levels) - 1).astype(jnp.float32) * tick_length
    for step in range(active_rows.shape[0]):
        now = (step + 1) * tick_length
        pred_pos, pred_vel = predict(positions, velocities, accelerations, jerks, now - last_time)
        rows = active_rows[step]
        targets = jnp.concatenate([pred_pos[:, rows], pred_vel[:, rows]], axis=0)
        step_counts = counts[step]
        own_count = step_counts[my_rank]
        inclusive = jnp.cumsum(step_counts).astype(jnp.int32)
        first = inclusive - step_counts
        place = jnp.arange(live_all, dtype=jnp.int32)
        owner = jnp.sum((inclusive[None, :] <= place[:, None]).astype(jnp.int32), axis=1)
        owner = jnp.minimum(owner, devices_all - 1)
        slot = owner * slot_cap + place - first[owner]
        gathered = lax.all_gather(targets[None], ("grp", "dev"), axis=0, tiled=True)
        flat = gathered.transpose(1, 0, 2).reshape(6, devices_all * slot_cap)
        compact = flat[:, slot]
        parts = []
        summed = None
        for c in range(chunks):
            piece = compact[:, c * chunk : (c + 1) * chunk]
            terms = block_terms(piece, pred_pos, pred_vel, mass, soft_sq)
            if summed is not None:
                terms, summed = lax.optimization_barrier((terms, summed))
                parts.append(summed)
            summed = lax.psum(terms, ("grp", "dev"))
        parts.append(summed)
        parts.append(jnp.zeros((6, slot_cap), jnp.float32))
        totals = jnp.concatenate(parts, axis=1)
        own = lax.dynamic_slice_in_dim(totals, first[my_rank], slot_cap, 1)
        span = now - last_time[rows]
        new_pos, new_vel = correct(
            positions[:, rows],
            velocities[:, rows],
            accelerations[:, rows],
            jerks[:, rows],
            own[:3],
            own[3:],
            span,
        )
        live = jnp.arange(slot_cap, dtype=jnp.int32) < own_count
        target = jnp.where(live, rows, star_dev)
        positions = positions.at[:, target].set(new_pos, mode="drop")
        velocities = velocities.at[:, target].set(new_vel, mode="drop")
        accelerations = accelerations.at[:, target].set(own[:3], mode="drop")
        jerks = jerks.at[:, target].set(own[3:], mode="drop")
        last_time = last_time.at[target].set(now, mode="drop")
    return (positions, velocities, accelerations, jerks)


def solution(mesh):
    placed = (
        P(None, ("grp", "dev")),
        P(None, ("grp", "dev")),
        P(None, ("grp", "dev")),
        P(None, ("grp", "dev")),
        P(("grp", "dev")),
        P(),
        P(None, ("grp", "dev")),
    )
    return jax.shard_map(
        shards,
        mesh=mesh,
        in_specs=placed,
        out_specs=(
            P(None, ("grp", "dev")),
            P(None, ("grp", "dev")),
            P(None, ("grp", "dev")),
            P(None, ("grp", "dev")),
        ),
        check_vma=False,
    )
```

profile of v0, /device:TPU:1, one launch (start us, length us, event | category | flops | bytes accessed | tf_op | source)
XLA Modules:
  0.0 1731.8 jit_solution(9103468403013295511)
XLA Ops:
  14.8 63.9 %all-gather.2 = f32[128,6,256]{2,1,0:T(8,128)S(1)} all-gather(f32[1,6,256]{2,1,0:T(8,128)S(1)} %maximum_bitcast_fusion), channel_id=2, replica_groups=mesh['grp'=8,'dev'=16] {'grp','dev'}, dimensions={0}, use_global_device_ids=true | all-gather | bytes 792576 | tf_op jit(solution)/shard_map/all_gather | solution.py:85
  90.3 97.2 %gather_fusion.6 = s32[16384]{0:T(1024)S(1)} fusion(s32[128]{0:T(128)S(1)} %get-tuple-element.734, s32[16384]{0:T(1024)S(1)} %broadcast_clamp_fusion.3), kind=kCustom, calls=%fused_computation.6 | custom fusion | bytes 196608 | tf_op jit(solution)/shard_map/gather | solution.py:84
  187.7 60.2 %gather_fusion.7 = f32[16384,6]{1,0:T(8,128)} fusion(f32[6,32768]{0,1:T(8,128)} %bitcast.632, s32[16384]{0:T(1024)S(1)} %broadcast_clamp_fusion.1), kind=kCustom, calls=%fused_computation.7 | custom fusion | bytes 851968 | tf_op jit(solution)/shard_map/gather | solution.py:87
  256.3 32.8 %while.81 = (s32[]{:T(128)}, f32[2,6,2048]{2,1,0:T(8,128)S(1)}, f32[3,1024]{1,0:T(4,128)S(1)}, f32[2,6,2048]{2,1,0:T(8,128)S(1)}, f32[3,1024]{1,0:T(4,128)S(1)},...) while((s32[]{:T(128)}, f32[2,6,2048]{2,1,0:T(8,128)S(1)}, ...), condition=%wide.region_17.18_spmd, body=%wide.region_10.17_spmd.sunk | while | flops 85970952 | bytes 499925 | solution.py:37
  256.4 16.2 fusion.187
  272.8 16.2 fusion.187
  294.7 32.8 %while.80 = (s32[]{:T(128)}, f32[2,6,2048]{2,1,0:T(8,128)S(1)}, f32[3,1024]{1,0:T(4,128)S(1)}, f32[2,6,2048]{2,1,0:T(8,128)S(1)}, f32[3,1024]{1,0:T(4,128)S(1)},...) while((s32[]{:T(128)}, f32[2,6,2048]{2,1,0:T(8,128)S(1)}, ...), condition=%wide.region_9.10_spmd, body=%wide.region_2.9_spmd.sunk | while | flops 85970952 | bytes 499925 | solution.py:37
  294.8 16.2 fusion.185
  311.2 16.2 fusion.185
  329.8 32.8 %while.82 = (s32[]{:T(128)}, f32[2,6,2048]{2,1,0:T(8,128)S(1)}, f32[3,1024]{1,0:T(4,128)S(1)}, f32[2,6,2048]{2,1,0:T(8,128)S(1)}, f32[3,1024]{1,0:T(4,128)S(1)},...) while((s32[]{:T(128)}, f32[2,6,2048]{2,1,0:T(8,128)S(1)}, ...), condition=%wide.region_26.27_spmd, body=%wide.region_19.26_spmd.sunk | while | flops 85970952 | bytes 499925 | solution.py:37
  329.9 16.2 fusion.189
  346.4 16.2 fusion.189
  363.3 32.9 %while.83 = (s32[]{:T(128)}, f32[2,6,2048]{2,1,0:T(8,128)S(1)}, f32[3,1024]{1,0:T(4,128)S(1)}, f32[2,6,2048]{2,1,0:T(8,128)S(1)}, f32[3,1024]{1,0:T(4,128)S(1)},...) while((s32[]{:T(128)}, f32[2,6,2048]{2,1,0:T(8,128)S(1)}, ...), condition=%wide.region_35.36_spmd, body=%wide.region_28.35_spmd.sunk | while | flops 85970952 | bytes 499925 | solution.py:37
  363.4 16.2 fusion.191
  379.9 16.2 fusion.191
  399.8 97.2 %gather_fusion.15 = s32[16384]{0:T(1024)S(1)} fusion(s32[128]{0:T(128)S(1)} %get-tuple-element.733, s32[16384]{0:T(1024)S(1)} %broadcast_clamp_fusion.2), kind=kCustom, calls=%fused_computation.15 | custom fusion | bytes 196608 | tf_op jit(solution)/shard_map/gather | solution.py:84
  509.3 137.8 %all-reduce.11.cloned.1.call-done = f32[6,4096]{1,0:T(8,128)} async-done(((f32[6,4096]{1,0:T(8,128)}), f32[6,4096]{1,0:T(8,128)}) %all-reduce.11.cloned.1.call-update) | async-done | bytes 98320 | tf_op jit(solution)/shard_map/psum | solution.py:96
  648.1 141.3 %all-reduce.13.cloned.1.call-done = f32[6,4096]{1,0:T(8,128)} async-done(((f32[6,4096]{1,0:T(8,128)}), f32[6,4096]{1,0:T(8,128)}) %all-reduce.13.cloned.1.call-update) | async-done | bytes 98320 | tf_op jit(solution)/shard_map/psum | solution.py:96
  790.4 141.8 %all-reduce.15.cloned.1.call-done = f32[6,4096]{1,0:T(8,128)} async-done(((f32[6,4096]{1,0:T(8,128)}), f32[6,4096]{1,0:T(8,128)}) %all-reduce.15.cloned.1.call-update) | async-done | bytes 98320 | tf_op jit(solution)/shard_map/psum | solution.py:96
  941.9 59.0 %all-gather.3 = f32[128,6,256]{2,1,0:T(8,128)S(1)} all-gather(f32[1,6,256]{2,1,0:T(8,128)S(1)} %maximum_bitcast_fusion.1), channel_id=3, replica_groups=mesh['grp'=8,'dev'=16] {'grp','dev'}, dimensions={0}, use_global_device_ids=true | all-gather | bytes 792576 | tf_op jit(solution)/shard_map/all_gather | solution.py:85
  1009.3 60.2 %gather_fusion.16 = f32[16384,6]{1,0:T(8,128)} fusion(f32[6,32768]{0,1:T(8,128)} %bitcast.633, s32[16384]{0:T(1024)S(1)} %broadcast_clamp_fusion), kind=kCustom, calls=%fused_computation.16 | custom fusion | bytes 851968 | tf_op jit(solution)/shard_map/gather | solution.py:87
  1077.9 32.8 %while.84 = (s32[]{:T(128)}, f32[2,6,2048]{2,1,0:T(8,128)S(1)}, f32[3,1024]{1,0:T(4,128)S(1)}, f32[2,6,2048]{2,1,0:T(8,128)S(1)}, f32[3,1024]{1,0:T(4,128)S(1)},...) while((s32[]{:T(128)}, f32[2,6,2048]{2,1,0:T(8,128)S(1)}, ...), condition=%wide.region_52.53_spmd, body=%wide.region_45.52_spmd.sunk | while | flops 85970952 | bytes 499925 | solution.py:37
  1113.6 34.0 %while.85 = (s32[]{:T(128)}, f32[2,6,2048]{2,1,0:T(8,128)}, f32[3,1024]{1,0:T(4,128)S(1)}, f32[2,6,2048]{2,1,0:T(8,128)S(1)}, f32[3,1024]{1,0:T(4,128)S(1)}, /*i...) while((s32[]{:T(128)}, f32[2,6,2048]{2,1,0:T(8,128)}, f32[3,1024]{1,0:T(4,128)S(1)}, ...), condition=%wide.region_60.61_spmd, body=%wide.region_53.60_spmd.sunk | while | flops 85970952 | bytes 483541 | solution.py:37
  1113.7 16.2 fusion.195
  1150.1 32.8 %while.86 = (s32[]{:T(128)}, f32[2,6,2048]{2,1,0:T(8,128)S(1)}, f32[3,1024]{1,0:T(4,128)S(1)}, f32[2,6,2048]{2,1,0:T(8,128)S(1)}, f32[3,1024]{1,0:T(4,128)S(1)},...) while((s32[]{:T(128)}, f32[2,6,2048]{2,1,0:T(8,128)S(1)}, ...), condition=%wide.region_69.70_spmd, body=%wide.region_62.69_spmd.sunk | while | flops 85970952 | bytes 499925 | solution.py:37
  1150.2 16.2 fusion.197
  1166.6 16.2 fusion.197
  1183.7 32.8 %while.87 = (s32[]{:T(128)}, f32[2,6,2048]{2,1,0:T(8,128)S(1)}, f32[3,1024]{1,0:T(4,128)S(1)}, f32[2,6,2048]{2,1,0:T(8,128)S(1)}, f32[3,1024]{1,0:T(4,128)S(1)},...) while((s32[]{:T(128)}, f32[2,6,2048]{2,1,0:T(8,128)S(1)}, ...), condition=%wide.region_78.79_spmd, body=%wide.region_71.78_spmd.sunk | while | flops 85970952 | bytes 499925 | solution.py:37
  1219.8 66.7 %all-reduce.17.cloned.1.call-done = f32[6,4096]{1,0:T(8,128)} async-done(((f32[6,4096]{1,0:T(8,128)}), f32[6,4096]{1,0:T(8,128)}) %all-reduce.17.cloned.1.call-update) | async-done | bytes 98320 | tf_op jit(solution)/shard_map/psum | solution.py:96
  1287.5 141.8 %all-reduce.19.cloned.1.call-done = f32[6,4096]{1,0:T(8,128)} async-done(((f32[6,4096]{1,0:T(8,128)}), f32[6,4096]{1,0:T(8,128)}) %all-reduce.19.cloned.1.call-update) | async-done | bytes 98320 | tf_op jit(solution)/shard_map/psum | solution.py:96
  1430.3 141.2 %all-reduce.21.cloned.1.call-done = f32[6,4096]{1,0:T(8,128)} async-done(((f32[6,4096]{1,0:T(8,128)}), f32[6,4096]{1,0:T(8,128)}) %all-reduce.21.cloned.1.call-update) | async-done | bytes 98320 | tf_op jit(solution)/shard_map/psum | solution.py:96
  1572.5 142.0 %all-reduce.23.cloned.1.call-done = f32[6,4096]{1,0:T(8,128)} async-done(((f32[6,4096]{1,0:T(8,128)}), f32[6,4096]{1,0:T(8,128)}) %all-reduce.23.cloned.1.call-update) | async-done | bytes 98320 | tf_op jit(solution)/shard_map/psum | solution.py:96
  (250 shorter events, 183.6 us)
Async XLA Ops:
  7.2 501.2 %all-reduce.9.cloned.1.call-start = ((), (), s32[]{:S(2)}) async-start(), calls=%async_computation | async-start | bytes 262144 | tf_op jit(solution)/shard_map/psum | solution.py:96
  78.7 11.5 copy-start.18
  289.1 0.6 copy-start.5
  289.8 357.4 %all-reduce.11.cloned.1.call-start = ((), (), s32[]{:S(2)}) async-start(), calls=%async_computation.1 | async-start | bytes 262144 | tf_op jit(solution)/shard_map/psum | solution.py:96
  327.5 2.3 copy-start.6
  362.7 0.7 copy-start.7
  396.2 100.8 %copy-start.8 = (f32[2,6,2048]{2,1,0:T(8,128)}, f32[2,6,2048]{2,1,0:T(8,128)S(1)}, u32[]{:S(2)}) copy-start(f32[2,6,2048]{2,1,0:T(8,128)S(1)} %get-tuple-element.238) | copy-start | bytes 294916
  397.6 543.1 %copy-start.15 = (s32[1024]{0:T(1024)}, s32[1024]{0:T(1024)S(1)}, u32[]{:S(2)}) copy-start(s32[1024]{0:T(1024)S(1)} %pad_clamp_fusion) | copy-start | bytes 12292
  399.7 99.4 %copy-start.11 = (f32[3,1024]{1,0:T(4,128)S(1)}, f32[3,1024]{1,0:T(4,128)}, u32[]{:S(2)}) copy-start(f32[3,1024]{1,0:T(4,128)} %param.23) | copy-start | bytes 36868
  399.7 99.6 %copy-start.12 = (f32[3,1024]{1,0:T(4,128)S(1)}, f32[3,1024]{1,0:T(4,128)}, u32[]{:S(2)}) copy-start(f32[3,1024]{1,0:T(4,128)} %param.25) | copy-start | bytes 36868
  399.7 99.8 %copy-start.13 = (f32[3,1024]{1,0:T(4,128)S(1)}, f32[3,1024]{1,0:T(4,128)}, u32[]{:S(2)}) copy-start(f32[3,1024]{1,0:T(4,128)} %param.24) | copy-start | bytes 36868
  399.7 100.7 %copy-start.14 = (f32[3,1024]{1,0:T(4,128)S(1)}, f32[3,1024]{1,0:T(4,128)}, u32[]{:S(2)}) copy-start(f32[3,1024]{1,0:T(4,128)} %param.26) | copy-start | bytes 36868
  508.4 281.0 %all-reduce.13.cloned.1.call-start = ((), (), s32[]{:S(2)}) async-start(), calls=%async_computation.2 | async-start | bytes 262144 | tf_op jit(solution)/shard_map/psum | solution.py:96
  647.2 285.0 %all-reduce.15.cloned.1.call-start = ((), (), s32[]{:S(2)}) async-start(), calls=%async_computation.3 | async-start | bytes 262144 | tf_op jit(solution)/shard_map/psum | solution.py:96
  789.4 497.1 %all-reduce.17.cloned.1.call-start = ((), (), s32[]{:S(2)}) async-start(), calls=%async_computation.4 | async-start | bytes 262144 | tf_op jit(solution)/shard_map/psum | solution.py:96
  934.7 74.5 %copy-start.2 = (f32[3,1024]{0,1:T(8,128)}, f32[3,1024]{0,1:T(8,128)S(1)}, u32[]{:S(2)}) copy-start(f32[3,1024]{0,1:T(8,128)S(1)} %scatter_fusion) | copy-start | bytes 36868
  936.3 73.0 %copy-start = (f32[3,1024]{0,1:T(8,128)}, f32[3,1024]{0,1:T(8,128)S(1)}, u32[]{:S(2)}) copy-start(f32[3,1024]{0,1:T(8,128)S(1)} %scatter_fusion.3) | copy-start | bytes 36868
  1110.7 2.9 copy-start.9
  1147.6 281.7 %all-reduce.19.cloned.1.call-start = ((), (), s32[]{:S(2)}) async-start(), calls=%async_computation.5 | async-start | bytes 262144 | tf_op jit(solution)/shard_map/psum | solution.py:96
  1183.0 0.7 copy-start.10
  1183.6 32.9 %copy-start.1 = (f32[3,1024]{0,1:T(8,128)S(1)}, f32[3,1024]{0,1:T(8,128)}, u32[]{:S(2)}) copy-start(f32[3,1024]{0,1:T(8,128)} %copy-done) | copy-start | bytes 36868
  1183.6 32.9 %copy-start.16 = (s32[1024]{0:T(1024)S(1)}, s32[1024]{0:T(1024)}, u32[]{:S(2)}) copy-start(s32[1024]{0:T(1024)} %copy-done.15) | copy-start | bytes 12292
  1183.6 34.3 %copy-start.3 = (f32[3,1024]{0,1:T(8,128)S(1)}, f32[3,1024]{0,1:T(8,128)}, u32[]{:S(2)}) copy-start(f32[3,1024]{0,1:T(8,128)} %copy-done.2) | copy-start | bytes 36868
  1183.6 531.7 %copy-start.19 = (f32[256]{0:T(256)S(1)}, f32[256]{0:T(256)}, u32[]{:S(2)}) copy-start(f32[256]{0:T(256)} %get-tuple-element.731) | copy-start | bytes 3076
  1183.6 531.7 %copy-start.20 = (f32[256]{0:T(256)S(1)}, f32[256]{0:T(256)}, u32[]{:S(2)}) copy-start(f32[256]{0:T(256)} %get-tuple-element.732) | copy-start | bytes 3076
  1183.7 531.9 %copy-start.17 = (s32[256,1]{0,1:T(1,128)S(1)}, s32[256,1]{0,1:T(1,128)}, u32[]{:S(2)}) copy-start(s32[256,1]{0,1:T(1,128)} %get-tuple-element.729) | copy-start | bytes 3076
  1216.5 355.0 %copy-start.4 = (f32[2,6,2048]{2,1,0:T(8,128)}, f32[2,6,2048]{2,1,0:T(8,128)S(1)}, u32[]{:S(2)}) copy-start(f32[2,6,2048]{2,1,0:T(8,128)S(1)} %get-tuple-element.248) | copy-start | bytes 294916
  1286.5 285.0 %all-reduce.21.cloned.1.call-start = ((), (), s32[]{:S(2)}) async-start(), calls=%async_computation.6 | async-start | bytes 262144 | tf_op jit(solution)/shard_map/psum | solution.py:96
  1429.3 285.1 %all-reduce.23.cloned.1.call-start = ((), (), s32[]{:S(2)}) async-start(), calls=%async_computation.7 | async-start | bytes 262144 | tf_op jit(solution)/shard_map/psum | solution.py:96
Sparse Core Ops, SparseCore 0:
  289.9 138.5 all-reduce.8
  508.5 138.5 all-reduce.10
  651.9 137.4 all-reduce.12
  794.7 137.4 all-reduce.14
  1147.8 138.6 all-reduce.16
  1291.8 137.4 all-reduce.18
  1434.0 137.4 all-reduce.20
  1577.0 137.4 all-reduce.22
where the time goes:
time: 1740 us; the launch traced here: 1730 us
  waiting for transfers between devices  913 us (52%)
  local copies, waits for them, and re-layouts  405 us (23%)
  other arithmetic  270 us (16%)
  blocking collectives  123 us (7%)
  between operations  19 us (1%)
    psum x8, waiting for transfers between devices, shards(): summed = lax.psum(terms, ('grp', 'dev'))  913 us
    reduce_sum x16, other arithmetic, pair_block(): jnp.sum(weight * (drift_z - along * gap_z), axis=1)  259 us
    gather x2, local copies, waits for them, and re-layouts, shards(): slot = owner * slot_cap + place - first[owner]  194 us
    all_gather x2, blocking collectives, shards(): gathered = lax.all_gather(targets[None], ('grp', 'dev'), axis=0, tiled=True)  123 us
    gather x2, local copies, waits for them, and re-layouts, shards(): compact = flat[:, slot]  120 us
  transfers between devices with their start and end apart: 8, of which 7 were waited for; matrix products, arithmetic and copies ran while one was open for 17% of the time, Pallas kernels for 0%

commit v1 on v0

--- a/solution.py
+++ b/solution.py
@@ -93,7 +93,7 @@
             if summed is not None:
                 terms, summed = lax.optimization_barrier((terms, summed))
                 parts.append(summed)
-            summed = lax.psum(terms, ("grp", "dev"))
+            summed = jnp.sum(lax.all_gather(terms, ("grp", "dev")), axis=0)
         parts.append(summed)
         parts.append(jnp.zeros((6, slot_cap), jnp.float32))
         totals = jnp.concatenate(parts, axis=1)

time: 1740 us -> 1220 us (0.70)
  waiting for transfers between devices: 913 us -> 336 us
  other arithmetic: 270 us -> 330 us
    psum x8 -> x0, waiting for transfers between devices: 913 us -> none  [shards(): summed = lax.psum(terms, ('grp', 'dev'))]
    all_gather x0 -> x8, waiting for transfers between devices: none -> 336 us  [shards(): summed = jnp.sum(lax.all_gather(terms, ('grp', 'dev')), axis=0)]
    reduce_sum x0 -> x8, other arithmetic: none -> 56.1 us  [shards(): summed = jnp.sum(lax.all_gather(terms, ('grp', 'dev')), axis=0)]
  transfers between devices with their start and end apart: 8 -> 8, of which waited for: 7 -> 7; matrix products, arithmetic and copies ran while one was open for 17% -> 27% of each run, Pallas kernels for 0% -> 0%
where the time goes in v1:
time: 1220 us; the launch traced here: 1210 us
  local copies, waits for them, and re-layouts  403 us (33%)
  waiting for transfers between devices  336 us (28%)
  other arithmetic  330 us (27%)
  blocking collectives  124 us (10%)
  between operations  19.1 us (2%)
    all_gather x8, waiting for transfers between devices, shards(): summed = jnp.sum(lax.all_gather(terms, ('grp', 'dev')), axis=0)  336 us
    reduce_sum x16, other arithmetic, pair_block(): jnp.sum(weight * (drift_z - along * gap_z), axis=1)  263 us
    gather x2, local copies, waits for them, and re-layouts, shards(): slot = owner * slot_cap + place - first[owner]  194 us
    all_gather x2, blocking collectives, shards(): gathered = lax.all_gather(targets[None], ('grp', 'dev'), axis=0, tiled=True)  124 us
    gather x2, local copies, waits for them, and re-layouts, shards(): compact = flat[:, slot]  120 us
    reduce_sum x8, other arithmetic, shards(): summed = jnp.sum(lax.all_gather(terms, ('grp', 'dev')), axis=0)  56.1 us
  transfers between devices with their start and end apart: 8, of which 7 were waited for; matrix products, arithmetic and copies ran while one was open for 27% of the time, Pallas kernels for 0%

profile of v1, /device:TPU:1, one launch (start us, length us, event | category | flops | bytes accessed | tf_op | source)
XLA Modules:
  0.0 1213.6 jit_solution(15277183723688861052)
XLA Ops:
  14.8 63.9 %all-gather.8 = f32[128,6,256]{2,1,0:T(8,128)S(1)} all-gather(f32[1,6,256]{2,1,0:T(8,128)S(1)} %maximum_bitcast_fusion), channel_id=2, replica_groups=mesh['grp'=8,'dev'=16] {'grp','dev'}, dimensions={0}, use_global_device_ids=true | all-gather | bytes 792576 | tf_op jit(solution)/shard_map/all_gather | solution.py:85
  90.3 97.2 %gather_fusion.6 = s32[16384]{0:T(1024)S(1)} fusion(s32[128]{0:T(128)S(1)} %get-tuple-element.734, s32[16384]{0:T(1024)S(1)} %broadcast_clamp_fusion.3), kind=kCustom, calls=%fused_computation.6 | custom fusion | bytes 196608 | tf_op jit(solution)/shard_map/gather | solution.py:84
  187.7 60.2 %gather_fusion.7 = f32[16384,6]{1,0:T(8,128)} fusion(f32[6,32768]{0,1:T(8,128)} %bitcast.638, s32[16384]{0:T(1024)S(1)} %broadcast_clamp_fusion.1), kind=kCustom, calls=%fused_computation.7 | custom fusion | bytes 851968 | tf_op jit(solution)/shard_map/gather | solution.py:87
  256.3 32.9 %while.81 = (s32[]{:T(128)}, f32[2,6,2048]{2,1,0:T(8,128)S(1)}, f32[3,1024]{1,0:T(4,128)S(1)}, f32[2,6,2048]{2,1,0:T(8,128)S(1)}, f32[3,1024]{1,0:T(4,128)S(1)},...) while((s32[]{:T(128)}, f32[2,6,2048]{2,1,0:T(8,128)S(1)}, ...), condition=%wide.region_17.18_spmd, body=%wide.region_10.17_spmd.sunk | while | flops 85970952 | bytes 499925 | solution.py:37
  256.4 16.2 %fusion.187 = (f32[2048]{0:T(1024)S(1)}, f32[2048]{0:T(1024)S(1)}, f32[2048]{0:T(1024)S(1)}, f32[2048]{0:T(1024)S(1)}, f32[2048]{0:T(1024)S(1)}, /*index=5*/f32[2048]{0:T(1024)S(1)}) fusion(f32[2048]{0:T(1024)S(1)} %bitcast.731, f32[1024]{0:T(1024)S(1)} %bitcast.779, f32[2048]{0:T(1024)S(1)} %bitcast.728, f32[1024]{0:T(1024)S(1)} %bitcast.782, ...), kind=kLoop, calls=%fused_computation.89.clone.1 | loop fusion | flops 85970944 | bytes 122880 | tf_op jit(solution)/shard_map/while/body/eval_jaxpr/reduce_sum | solution.py:28
  292.3 32.9 %while.80 = (s32[]{:T(128)}, f32[2,6,2048]{2,1,0:T(8,128)S(1)}, f32[3,1024]{1,0:T(4,128)S(1)}, f32[2,6,2048]{2,1,0:T(8,128)S(1)}, f32[3,1024]{1,0:T(4,128)S(1)},...) while((s32[]{:T(128)}, f32[2,6,2048]{2,1,0:T(8,128)S(1)}, ...), condition=%wide.region_9.10_spmd, body=%wide.region_2.9_spmd.sunk | while | flops 85970952 | bytes 499925 | solution.py:37
  308.8 16.2 %fusion.185 = (f32[2048]{0:T(1024)S(1)}, f32[2048]{0:T(1024)S(1)}, f32[2048]{0:T(1024)S(1)}, f32[2048]{0:T(1024)S(1)}, f32[2048]{0:T(1024)S(1)}, /*index=5*/f32[2048]{0:T(1024)S(1)}) fusion(f32[2048]{0:T(1024)S(1)} %bitcast.737, f32[1024]{0:T(1024)S(1)} %bitcast.785, f32[2048]{0:T(1024)S(1)} %bitcast.734, f32[1024]{0:T(1024)S(1)} %bitcast.788, ...), kind=kLoop, calls=%fused_computation.49.clone.1 | loop fusion | flops 85970944 | bytes 122880 | tf_op jit(solution)/shard_map/while/body/eval_jaxpr/reduce_sum | solution.py:28
  325.2 44.1 %all-gather.25.cloned.1.call-done = f32[128,6,4096]{2,1,0:T(8,128)} async-done(((f32[1,6,4096]{2,1,0:T(8,128)}), f32[128,6,4096]{2,1,0:T(8,128)}) %all-gather.25.cloned.1.call-update) | async-done | bytes 12582928 | tf_op jit(solution)/shard_map/all_gather | solution.py:96
  378.5 32.9 %while.82 = (s32[]{:T(128)}, f32[2,6,2048]{2,1,0:T(8,128)S(1)}, f32[3,1024]{1,0:T(4,128)S(1)}, f32[2,6,2048]{2,1,0:T(8,128)S(1)}, f32[3,1024]{1,0:T(4,128)S(1)},...) while((s32[]{:T(128)}, f32[2,6,2048]{2,1,0:T(8,128)S(1)}, ...), condition=%wide.region_26.27_spmd, body=%wide.region_19.26_spmd.sunk | while | flops 85970952 | bytes 499925 | solution.py:37
  378.6 16.2 %fusion.189 = (f32[2048]{0:T(1024)S(1)}, f32[2048]{0:T(1024)S(1)}, f32[2048]{0:T(1024)S(1)}, f32[2048]{0:T(1024)S(1)}, f32[2048]{0:T(1024)S(1)}, /*index=5*/f32[2048]{0:T(1024)S(1)}) fusion(f32[2048]{0:T(1024)S(1)} %bitcast.743, f32[1024]{0:T(1024)S(1)} %bitcast.791, f32[2048]{0:T(1024)S(1)} %bitcast.740, f32[1024]{0:T(1024)S(1)} %bitcast.794, ...), kind=kLoop, calls=%fused_computation.129.clone.1 | loop fusion | flops 85970944 | bytes 122880 | tf_op jit(solution)/shard_map/while/body/eval_jaxpr/reduce_sum | solution.py:28
  411.4 44.8 %all-gather.29.cloned.1.call-done = f32[128,6,4096]{2,1,0:T(8,128)} async-done(((f32[1,6,4096]{2,1,0:T(8,128)}), f32[128,6,4096]{2,1,0:T(8,128)}) %all-gather.29.cloned.1.call-update) | async-done | bytes 12582928 | tf_op jit(solution)/shard_map/all_gather | solution.py:96
  463.9 32.9 %while.83 = (s32[]{:T(128)}, f32[2,6,2048]{2,1,0:T(8,128)S(1)}, f32[3,1024]{1,0:T(4,128)S(1)}, f32[2,6,2048]{2,1,0:T(8,128)S(1)}, f32[3,1024]{1,0:T(4,128)S(1)},...) while((s32[]{:T(128)}, f32[2,6,2048]{2,1,0:T(8,128)S(1)}, ...), condition=%wide.region_35.36_spmd, body=%wide.region_28.35_spmd.sunk | while | flops 85970952 | bytes 499925 | solution.py:37
  496.8 46.4 %all-gather.31.cloned.1.call-done = f32[128,6,4096]{2,1,0:T(8,128)} async-done(((f32[1,6,4096]{2,1,0:T(8,128)}), f32[128,6,4096]{2,1,0:T(8,128)}) %all-gather.31.cloned.1.call-update) | async-done | bytes 12582928 | tf_op jit(solution)/shard_map/all_gather | solution.py:96
  561.0 97.2 %gather_fusion.15 = s32[16384]{0:T(1024)S(1)} fusion(s32[128]{0:T(128)S(1)} %get-tuple-element.733, s32[16384]{0:T(1024)S(1)} %broadcast_clamp_fusion.2), kind=kCustom, calls=%fused_computation.15 | custom fusion | bytes 196608 | tf_op jit(solution)/shard_map/gather | solution.py:84
  675.6 60.3 %all-gather.12 = f32[128,6,256]{2,1,0:T(8,128)S(1)} all-gather(f32[1,6,256]{2,1,0:T(8,128)S(1)} %maximum_bitcast_fusion.1), channel_id=6, replica_groups=mesh['grp'=8,'dev'=16] {'grp','dev'}, dimensions={0}, use_global_device_ids=true | all-gather | bytes 792576 | tf_op jit(solution)/shard_map/all_gather | solution.py:85
  744.3 60.2 %gather_fusion.16 = f32[16384,6]{1,0:T(8,128)} fusion(f32[6,32768]{0,1:T(8,128)} %bitcast.639, s32[16384]{0:T(1024)S(1)} %broadcast_clamp_fusion), kind=kCustom, calls=%fused_computation.16 | custom fusion | bytes 851968 | tf_op jit(solution)/shard_map/gather | solution.py:87
  812.9 35.4 %while.85 = (s32[]{:T(128)}, f32[2,6,2048]{2,1,0:T(8,128)S(1)}, f32[3,1024]{1,0:T(4,128)S(1)}, f32[2,6,2048]{2,1,0:T(8,128)S(1)}, f32[3,1024]{1,0:T(4,128)S(1)},...) while((s32[]{:T(128)}, f32[2,6,2048]{2,1,0:T(8,128)S(1)}, ...), condition=%wide.region_60.61_spmd, body=%wide.region_53.60_spmd.sunk | while | flops 85970952 | bytes 499925 | solution.py:37
  813.0 16.8 %fusion.195 = (f32[2048]{0:T(1024)S(1)}, f32[2048]{0:T(1024)S(1)}, f32[2048]{0:T(1024)S(1)}, f32[2048]{0:T(1024)S(1)}, f32[2048]{0:T(1024)S(1)}, /*index=5*/f32[2048]{0:T(1024)}) fusion(f32[2048]{0:T(1024)S(1)} %bitcast.755, f32[1024]{0:T(1024)S(1)} %bitcast.803, f32[2048]{0:T(1024)S(1)} %bitcast.752, f32[1024]{0:T(1024)S(1)} %bitcast.806, ...), kind=kLoop, calls=%fused_computation.249.clone.1 | loop fusion | flops 85970944 | bytes 122880 | tf_op jit(solution)/shard_map/while/body/eval_jaxpr/reduce_sum | solution.py:28
  830.7 16.8 %fusion.195 = (f32[2048]{0:T(1024)S(1)}, f32[2048]{0:T(1024)S(1)}, f32[2048]{0:T(1024)S(1)}, f32[2048]{0:T(1024)S(1)}, f32[2048]{0:T(1024)S(1)}, /*index=5*/f32[2048]{0:T(1024)}) fusion(f32[2048]{0:T(1024)S(1)} %bitcast.755, f32[1024]{0:T(1024)S(1)} %bitcast.803, f32[2048]{0:T(1024)S(1)} %bitcast.752, f32[1024]{0:T(1024)S(1)} %bitcast.806, ...), kind=kLoop, calls=%fused_computation.249.clone.1 | loop fusion | flops 85970944 | bytes 122880 | tf_op jit(solution)/shard_map/while/body/eval_jaxpr/reduce_sum | solution.py:28
  851.2 35.4 %while.84 = (s32[]{:T(128)}, f32[2,6,2048]{2,1,0:T(8,128)S(1)}, f32[3,1024]{1,0:T(4,128)S(1)}, f32[2,6,2048]{2,1,0:T(8,128)S(1)}, f32[3,1024]{1,0:T(4,128)S(1)},...) while((s32[]{:T(128)}, f32[2,6,2048]{2,1,0:T(8,128)S(1)}, ...), condition=%wide.region_52.53_spmd, body=%wide.region_45.52_spmd.sunk | while | flops 85970952 | bytes 499925 | solution.py:37
  851.3 16.8 %fusion.193 = (f32[2048]{0:T(1024)S(1)}, f32[2048]{0:T(1024)S(1)}, f32[2048]{0:T(1024)S(1)}, f32[2048]{0:T(1024)S(1)}, f32[2048]{0:T(1024)S(1)}, /*index=5*/f32[2048]{0:T(1024)}) fusion(f32[2048]{0:T(1024)S(1)} %bitcast.761, f32[1024]{0:T(1024)S(1)} %bitcast.809, f32[2048]{0:T(1024)S(1)} %bitcast.758, f32[1024]{0:T(1024)S(1)} %bitcast.812, ...), kind=kLoop, calls=%fused_computation.209.clone.1 | loop fusion | flops 85970944 | bytes 122880 | tf_op jit(solution)/shard_map/while/body/eval_jaxpr/reduce_sum | solution.py:28
  869.0 16.8 %fusion.193 = (f32[2048]{0:T(1024)S(1)}, f32[2048]{0:T(1024)S(1)}, f32[2048]{0:T(1024)S(1)}, f32[2048]{0:T(1024)S(1)}, f32[2048]{0:T(1024)S(1)}, /*index=5*/f32[2048]{0:T(1024)}) fusion(f32[2048]{0:T(1024)S(1)} %bitcast.761, f32[1024]{0:T(1024)S(1)} %bitcast.809, f32[2048]{0:T(1024)S(1)} %bitcast.758, f32[1024]{0:T(1024)S(1)} %bitcast.812, ...), kind=kLoop, calls=%fused_computation.209.clone.1 | loop fusion | flops 85970944 | bytes 122880 | tf_op jit(solution)/shard_map/while/body/eval_jaxpr/reduce_sum | solution.py:28
  887.3 41.5 %all-gather.27.cloned.1.call-done = f32[128,6,4096]{2,1,0:T(8,128)} async-done(((f32[1,6,4096]{2,1,0:T(8,128)}), f32[128,6,4096]{2,1,0:T(8,128)}) %all-gather.27.cloned.1.call-update) | async-done | bytes 12582928 | tf_op jit(solution)/shard_map/all_gather | solution.py:96
  938.9 36.6 %while.86 = (s32[]{:T(128)}, f32[2,6,2048]{2,1,0:T(8,128)}, f32[3,1024]{1,0:T(4,128)S(1)}, f32[2,6,2048]{2,1,0:T(8,128)S(1)}, f32[3,1024]{1,0:T(4,128)S(1)}, /*i...) while((s32[]{:T(128)}, f32[2,6,2048]{2,1,0:T(8,128)}, f32[3,1024]{1,0:T(4,128)S(1)}, ...), condition=%wide.region_69.70_spmd, body=%wide.region_62.69_spmd.sunk | while | flops 85970952 | bytes 483541 | solution.py:37
  939.0 16.8 %fusion.197 = (f32[2048]{0:T(1024)S(1)}, f32[2048]{0:T(1024)S(1)}, f32[2048]{0:T(1024)S(1)}, f32[2048]{0:T(1024)S(1)}, f32[2048]{0:T(1024)S(1)}, /*index=5*/f32[2048]{0:T(1024)}) fusion(f32[2048]{0:T(1024)S(1)} %bitcast.767, f32[1024]{0:T(1024)S(1)} %bitcast.815, f32[2048]{0:T(1024)S(1)} %bitcast.764, f32[1024]{0:T(1024)S(1)} %bitcast.818, ...), kind=kLoop, calls=%fused_computation.289.clone.1 | loop fusion | flops 85970944 | bytes 122880 | tf_op jit(solution)/shard_map/while/body/eval_jaxpr/reduce_sum | solution.py:28
  957.3 16.8 %fusion.197 = (f32[2048]{0:T(1024)S(1)}, f32[2048]{0:T(1024)S(1)}, f32[2048]{0:T(1024)S(1)}, f32[2048]{0:T(1024)S(1)}, f32[2048]{0:T(1024)S(1)}, /*index=5*/f32[2048]{0:T(1024)}) fusion(f32[2048]{0:T(1024)S(1)} %bitcast.767, f32[1024]{0:T(1024)S(1)} %bitcast.815, f32[2048]{0:T(1024)S(1)} %bitcast.764, f32[1024]{0:T(1024)S(1)} %bitcast.818, ...), kind=kLoop, calls=%fused_computation.289.clone.1 | loop fusion | flops 85970944 | bytes 122880 | tf_op jit(solution)/shard_map/while/body/eval_jaxpr/reduce_sum | solution.py:28
  975.5 40.3 %all-gather.35.cloned.1.call-done = f32[128,6,4096]{2,1,0:T(8,128)} async-done(((f32[1,6,4096]{2,1,0:T(8,128)}), f32[128,6,4096]{2,1,0:T(8,128)}) %all-gather.35.cloned.1.call-update) | async-done | bytes 12582928 | tf_op jit(solution)/shard_map/all_gather | solution.py:96
  1024.1 32.9 %while.87 = (s32[]{:T(128)}, f32[2,6,2048]{2,1,0:T(8,128)S(1)}, f32[3,1024]{1,0:T(4,128)S(1)}, f32[2,6,2048]{2,1,0:T(8,128)S(1)}, f32[3,1024]{1,0:T(4,128)S(1)},...) while((s32[]{:T(128)}, f32[2,6,2048]{2,1,0:T(8,128)S(1)}, ...), condition=%wide.region_78.79_spmd, body=%wide.region_71.78_spmd.sunk | while | flops 85970952 | bytes 499925 | solution.py:37
  1024.2 16.2 %fusion.199 = (f32[2048]{0:T(1024)S(1)}, f32[2048]{0:T(1024)S(1)}, f32[2048]{0:T(1024)S(1)}, f32[2048]{0:T(1024)S(1)}, f32[2048]{0:T(1024)S(1)}, /*index=5*/f32[2048]{0:T(1024)S(1)}) fusion(f32[2048]{0:T(1024)S(1)} %bitcast.773, f32[1024]{0:T(1024)S(1)} %bitcast.821, f32[2048]{0:T(1024)S(1)} %bitcast.770, f32[1024]{0:T(1024)S(1)} %bitcast.824, ...), kind=kLoop, calls=%fused_computation.329.clone.1 | loop fusion | flops 85970944 | bytes 122880 | tf_op jit(solution)/shard_map/while/body/eval_jaxpr/reduce_sum | solution.py:28
  1040.6 16.2 %fusion.199 = (f32[2048]{0:T(1024)S(1)}, f32[2048]{0:T(1024)S(1)}, f32[2048]{0:T(1024)S(1)}, f32[2048]{0:T(1024)S(1)}, f32[2048]{0:T(1024)S(1)}, /*index=5*/f32[2048]{0:T(1024)S(1)}) fusion(f32[2048]{0:T(1024)S(1)} %bitcast.773, f32[1024]{0:T(1024)S(1)} %bitcast.821, f32[2048]{0:T(1024)S(1)} %bitcast.770, f32[1024]{0:T(1024)S(1)} %bitcast.824, ...), kind=kLoop, calls=%fused_computation.329.clone.1 | loop fusion | flops 85970944 | bytes 122880 | tf_op jit(solution)/shard_map/while/body/eval_jaxpr/reduce_sum | solution.py:28
  1057.0 46.3 %all-gather.37.cloned.1.call-done = f32[128,6,4096]{2,1,0:T(8,128)} async-done(((f32[1,6,4096]{2,1,0:T(8,128)}), f32[128,6,4096]{2,1,0:T(8,128)}) %all-gather.37.cloned.1.call-update) | async-done | bytes 12582928 | tf_op jit(solution)/shard_map/all_gather | solution.py:96
  1117.6 72.7 %all-gather.39.cloned.1.call-done = f32[128,6,4096]{2,1,0:T(8,128)} async-done(((f32[1,6,4096]{2,1,0:T(8,128)}), f32[128,6,4096]{2,1,0:T(8,128)}) %all-gather.39.cloned.1.call-update) | async-done | bytes 12582928 | tf_op jit(solution)/shard_map/all_gather | solution.py:96
  (256 shorter events, 237.0 us)
Async XLA Ops:
  7.2 362.1 %all-gather.25.cloned.1.call-start = ((), (), s32[]{:S(2)}) async-start(), calls=%async_computation | async-start | bytes 16908288 | tf_op jit(solution)/shard_map/all_gather | solution.py:96
  78.7 11.5 copy-start.19
  289.2 0.7 copy-start.5
  289.8 166.4 %all-gather.29.cloned.1.call-start = ((), (), s32[]{:S(2)}) async-start(), calls=%async_computation.2 | async-start | bytes 16908288 | tf_op jit(solution)/shard_map/all_gather | solution.py:96
  325.2 51.0 %copy-start.6 = (f32[2,6,2048]{2,1,0:T(8,128)}, f32[2,6,2048]{2,1,0:T(8,128)S(1)}, u32[]{:S(2)}) copy-start(f32[2,6,2048]{2,1,0:T(8,128)S(1)} %get-tuple-element.232) | copy-start | bytes 294916
  376.2 166.9 %all-gather.31.cloned.1.call-start = ((), (), s32[]{:S(2)}) async-start(), calls=%async_computation.3 | async-start | bytes 16908288 | tf_op jit(solution)/shard_map/all_gather | solution.py:96
  411.4 51.8 %copy-start.7 = (f32[2,6,2048]{2,1,0:T(8,128)}, f32[2,6,2048]{2,1,0:T(8,128)S(1)}, u32[]{:S(2)}) copy-start(f32[2,6,2048]{2,1,0:T(8,128)S(1)} %get-tuple-element.235) | copy-start | bytes 294916
  463.2 196.7 %all-gather.33.cloned.1.call-start = ((), (), s32[]{:S(2)}) async-start(), calls=%async_computation.4 | async-start | bytes 16908288 | tf_op jit(solution)/shard_map/all_gather | solution.py:96
  496.7 53.3 %copy-start.8 = (f32[2,6,2048]{2,1,0:T(8,128)}, f32[2,6,2048]{2,1,0:T(8,128)S(1)}, u32[]{:S(2)}) copy-start(f32[2,6,2048]{2,1,0:T(8,128)S(1)} %get-tuple-element.238) | copy-start | bytes 294916
  496.8 53.6 %copy-start.12 = (f32[3,1024]{1,0:T(4,128)S(1)}, f32[3,1024]{1,0:T(4,128)}, u32[]{:S(2)}) copy-start(f32[3,1024]{1,0:T(4,128)} %param.23) | copy-start | bytes 36868
  496.8 53.9 %copy-start.13 = (f32[3,1024]{1,0:T(4,128)S(1)}, f32[3,1024]{1,0:T(4,128)}, u32[]{:S(2)}) copy-start(f32[3,1024]{1,0:T(4,128)} %param.25) | copy-start | bytes 36868
  496.8 54.1 %copy-start.14 = (f32[3,1024]{1,0:T(4,128)S(1)}, f32[3,1024]{1,0:T(4,128)}, u32[]{:S(2)}) copy-start(f32[3,1024]{1,0:T(4,128)} %param.24) | copy-start | bytes 36868
  496.8 54.9 %copy-start.15 = (f32[3,1024]{1,0:T(4,128)S(1)}, f32[3,1024]{1,0:T(4,128)}, u32[]{:S(2)}) copy-start(f32[3,1024]{1,0:T(4,128)} %param.26) | copy-start | bytes 36868
  550.1 378.7 %all-gather.27.cloned.1.call-start = ((), (), s32[]{:S(2)}) async-start(), calls=%async_computation.1 | async-start | bytes 16908288 | tf_op jit(solution)/shard_map/all_gather | solution.py:96
  659.6 14.9 %copy-start.16 = (s32[1024]{0:T(1024)}, s32[1024]{0:T(1024)S(1)}, u32[]{:S(2)}) copy-start(s32[1024]{0:T(1024)S(1)} %pad_clamp_fusion) | copy-start | bytes 12292
  668.5 75.8 %copy-start.2 = (f32[3,1024]{0,1:T(8,128)}, f32[3,1024]{0,1:T(8,128)S(1)}, u32[]{:S(2)}) copy-start(f32[3,1024]{0,1:T(8,128)S(1)} %scatter_fusion) | copy-start | bytes 36868
  670.0 74.2 %copy-start = (f32[3,1024]{0,1:T(8,128)}, f32[3,1024]{0,1:T(8,128)S(1)}, u32[]{:S(2)}) copy-start(f32[3,1024]{0,1:T(8,128)S(1)} %scatter_fusion.3) | copy-start | bytes 36868
  848.3 0.6 copy-start.9
  848.9 166.8 %all-gather.35.cloned.1.call-start = ((), (), s32[]{:S(2)}) async-start(), calls=%async_computation.5 | async-start | bytes 16908288 | tf_op jit(solution)/shard_map/all_gather | solution.py:96
  886.6 0.7 copy-start.10
  935.8 167.5 %all-gather.37.cloned.1.call-start = ((), (), s32[]{:S(2)}) async-start(), calls=%async_computation.6 | async-start | bytes 16908288 | tf_op jit(solution)/shard_map/all_gather | solution.py:96
  1023.4 166.9 %all-gather.39.cloned.1.call-start = ((), (), s32[]{:S(2)}) async-start(), calls=%async_computation.7 | async-start | bytes 16908288 | tf_op jit(solution)/shard_map/all_gather | solution.py:96
  1056.9 53.3 %copy-start.11 = (f32[2,6,2048]{2,1,0:T(8,128)}, f32[2,6,2048]{2,1,0:T(8,128)S(1)}, u32[]{:S(2)}) copy-start(f32[2,6,2048]{2,1,0:T(8,128)S(1)} %get-tuple-element.248) | copy-start | bytes 294916
  1056.9 55.2 %copy-start.17 = (s32[1024]{0:T(1024)S(1)}, s32[1024]{0:T(1024)}, u32[]{:S(2)}) copy-start(s32[1024]{0:T(1024)} %copy-done.16) | copy-start | bytes 12292
  1057.0 57.3 %copy-start.1 = (f32[3,1024]{0,1:T(8,128)S(1)}, f32[3,1024]{0,1:T(8,128)}, u32[]{:S(2)}) copy-start(f32[3,1024]{0,1:T(8,128)} %copy-done) | copy-start | bytes 36868
  1057.0 58.7 %copy-start.3 = (f32[3,1024]{0,1:T(8,128)S(1)}, f32[3,1024]{0,1:T(8,128)}, u32[]{:S(2)}) copy-start(f32[3,1024]{0,1:T(8,128)} %copy-done.2) | copy-start | bytes 36868
  1057.0 60.6 %copy-start.4 = (f32[6,4096]{1,0:T(8,128)S(1)}, f32[6,4096]{1,0:T(8,128)}, u32[]{:S(2)}) copy-start(f32[6,4096]{1,0:T(8,128)} %reduce_sum.529) | copy-start | bytes 294916
  1117.6 79.9 %copy-start.18 = (s32[256,1]{0,1:T(1,128)S(1)}, s32[256,1]{0,1:T(1,128)}, u32[]{:S(2)}) copy-start(s32[256,1]{0,1:T(1,128)} %get-tuple-element.729) | copy-start | bytes 3076
Sparse Core Ops, SparseCore 0:
  290.0 79.2 all-gather.24
  376.4 79.8 all-gather.28
  463.3 79.8 all-gather.30
  550.2 79.8 all-gather.32
  849.1 79.7 all-gather.26
  935.9 79.8 all-gather.34
  1023.5 79.8 all-gather.36
  1110.4 79.8 all-gather.38
